TPU v7x, 32 devices: a whole 2x2x4 slice. The times are simulated.
32 devices in a mesh: grp: 1, seq: 4 (over z), dp: 4 (over y, x), head: 2 (over core).
Axes of the slice: x: 2, y: 2, z: 4, core: 2. Of those that a mesh axis runs over, the one named last changes fastest.
Arguments:
- tokens_in: bfloat16 [4, 1024, 4096], P(('grp', 'dp'), 'seq'), may hold values from -6 to 6
- positions: int32 [4, 1024], P(('grp', 'dp'), 'seq'), may hold values from 0 to 1023, as said below
- doc_start: int32 [4, 1024], P(('grp', 'dp'), 'seq'), may hold values from 0 to 1, as said below
- feature_weight: bfloat16 [4096, 4096], P(('seq', 'dp'), 'head'), may hold values from -0.09375 to 0.09375
- state_weight: bfloat16 [4096, 128], P(('seq', 'dp')), may hold values from -0.01171875 to 0.01171875
- step_weight: bfloat16 [4096, 32], P(('seq', 'dp'), 'head'), may hold values from -0.09375 to 0.09375
- step_bias: float32 [32], P('head'), may hold values from -1 to 0.5
- decay_log: float32 [32], P('head')
- skip_gain: float32 [32], P('head'), may hold values from 0.4 to 1.9
- norm_gain: float32 [4096], P('head'), may hold values from 0.5 to 1.5
Outputs:
- mixed: bfloat16 [4, 1024, 4096], P(('grp', 'dp'), 'seq', 'head')
Inputs may be any that keep to these rules, and one draw needn't show every extreme that they name: Each sequence's rows carry every position once. Cut each device's 256 rows into 4 equal slots in order: the positions of slot k all lie in [k * 256, (k + 1) * 256). `doc_start`: position 0 of every sequence holds 1; a sequence holds at most 4 ones.
All inputs are finite; a program needn't handle non-finite values.
Results may differ from a plain program's by a relative error of at most 0.0062.
Values may be sent and summed in bfloat16 or wider, within the bound.
No kernel may reach another device: no remote copies, remote signals or barrier semaphores. Data moves between devices by JAX's collectives and lax.ppermute only.
A program may use at most 128 MiB of HBM per device.

v0:
```python
import jax
import jax.numpy as jnp
from jax import lax
from jax.sharding import PartitionSpec as P


def entering(value, axis, combine, identity, reverse):
    devices, here = (lax.axis_size(axis), lax.axis_index(axis))
    everything = jax.tree.map(lambda part: lax.all_gather(part, axis), value)
    start = jax.tree.map(
        lambda part, zero: jnp.broadcast_to(jnp.asarray(zero, part.dtype), part.shape),
        value,
        identity,
    )

    def lap(k, before):
        at = devices - 1 - k if reverse else k
        reached = at > here if reverse else at < here
        new = combine(before, jax.tree.map(lambda part: part[at], everything))
        return jax.tree.map(lambda a, b: jnp.where(reached, a, b), new, before)

    return lax.fori_loop(0, devices, lap, start)


def project_rows(features, feature_weight, state_weight, step_weight):
    return (
        jnp.dot(
            features,
            lax.all_gather(feature_weight, ("seq", "dp"), axis=0, tiled=True),
            preferred_element_type=jnp.float32,
        ).astype(jnp.bfloat16),
        jnp.dot(
            features,
            lax.all_gather(state_weight, ("seq", "dp"), axis=0, tiled=True),
            preferred_element_type=jnp.float32,
        ).astype(jnp.bfloat16),
        jnp.dot(
            features,
            lax.all_gather(step_weight, ("seq", "dp"), axis=0, tiled=True),
            preferred_element_type=jnp.float32,
        ).astype(jnp.bfloat16),
    )


def local_order(moved_positions, row_count):
    shard_index = lax.axis_index("seq")
    offsets = moved_positions - shard_index * row_count
    return (
        jnp.zeros((row_count,), jnp.int32).at[offsets].set(jnp.arange(row_count, dtype=jnp.int32))
    )


def head_terms(inputs, scores, same_doc, doc_index, b_float):
    cum_head, step_head, x_head = inputs
    decay = jnp.exp(-jnp.abs(cum_head[:, None] - cum_head[None, :])) * same_doc
    mixing = scores * decay * step_head[None, :]
    x_float = x_head.astype(jnp.float32)
    y_local = jnp.dot(mixing, x_float, precision=lax.Precision.HIGHEST)
    end_weight = jnp.exp(cum_head[-1] - cum_head) * (doc_index == doc_index[-1]) * step_head
    begin_weight = jnp.exp(cum_head) * (doc_index == 0) * step_head
    state_end = jnp.dot((b_float * end_weight[:, None]).T, x_float, precision=lax.Precision.HIGHEST)
    state_begin = jnp.dot(
        (b_float * begin_weight[:, None]).T, x_float, precision=lax.Precision.HIGHEST
    )
    return (y_local, state_end, state_begin)


def link(earlier, later):
    return (earlier[0] * later[0], later[0][:, None, None] * earlier[1] + later[1])


def per_device(
    tokens_in,
    positions,
    doc_start,
    feature_weight,
    state_weight,
    step_weight,
    step_bias,
    decay_log,
    skip_gain,
    norm_gain,
):
    row_count = tokens_in.shape[1]
    moved_rows, moved_positions = (
        lax.all_to_all(tokens_in, "seq", split_axis=1, concat_axis=1, tiled=True),
        lax.all_to_all(positions, "seq", split_axis=1, concat_axis=1, tiled=True),
    )
    inverse = local_order(moved_positions[0], row_count)
    features = moved_rows[0][inverse]
    x_proj, bc_proj, step_raw = project_rows(features, feature_weight, state_weight, step_weight)
    head_count = step_bias.shape[0]
    head_size = x_proj.shape[1] // head_count
    state_size = bc_proj.shape[1] // 2
    b_float = bc_proj[:, :state_size].astype(jnp.float32)
    c_float = bc_proj[:, state_size:].astype(jnp.float32)
    step_size = jax.nn.softplus(step_raw.astype(jnp.float32) + step_bias[None, :])
    log_decay = -jnp.exp(decay_log)[None, :] * step_size
    cum_decay = jnp.cumsum(log_decay, axis=0)
    doc_index = jnp.cumsum(doc_start[0], axis=0)
    scores = jnp.dot(
        bc_proj[:, state_size:], bc_proj[:, :state_size].T, preferred_element_type=jnp.float32
    )
    places = jnp.arange(row_count, dtype=jnp.int32)
    same_doc = (
        (doc_index[:, None] == doc_index[None, :]) & (places[:, None] != places[None, :])
    ).astype(jnp.float32)
    heads_x = x_proj.reshape(row_count, head_count, head_size).transpose(1, 0, 2)
    y_local, state_end, state_begin = lax.map(
        lambda item: head_terms(item, scores, same_doc, doc_index, b_float),
        (cum_decay.T, step_size.T, heads_x),
    )
    carry_gain = jnp.exp(cum_decay[-1]) * (doc_index[-1] == 0)
    identity = (
        jnp.ones((head_count,), jnp.float32),
        jnp.zeros((head_count, state_size, head_size), jnp.float32),
    )
    prefix = entering((carry_gain, state_end), "seq", link, identity, False)
    suffix = entering((carry_gain, state_begin), "seq", link, identity, True)
    left_gate = jnp.exp(cum_decay) * (doc_index == 0)[:, None]
    right_gate = jnp.exp(cum_decay[-1][None, :] - cum_decay) * (doc_index == doc_index[-1])[:, None]
    from_left = jnp.einsum("tn,hnp->thp", c_float, prefix[1], precision=lax.Precision.HIGHEST)
    from_right = jnp.einsum("tn,hnp->thp", c_float, suffix[1], precision=lax.Precision.HIGHEST)
    direct = x_proj.reshape(row_count, head_count, head_size).astype(jnp.float32)
    mixer = (
        y_local.transpose(1, 0, 2)
        + left_gate[:, :, None] * from_left
        + right_gate[:, :, None] * from_right
        + skip_gain[None, :, None] * direct
    )
    mixer_rows = mixer.reshape(row_count, head_count * head_size)
    square_sum = lax.psum(jnp.sum(mixer_rows * mixer_rows, axis=1), "head")
    full_width = mixer_rows.shape[1] * lax.axis_size("head")
    inv_scale = lax.rsqrt(square_sum / full_width + 1e-05)
    return (mixer_rows * inv_scale[:, None] * norm_gain[None, :]).astype(jnp.bfloat16)[None]


def solution(mesh):
    placed = (
        P(("grp", "dp"), "seq", None),
        P(("grp", "dp"), "seq"),
        P(("grp", "dp"), "seq"),
        P(("seq", "dp"), "head"),
        P(("seq", "dp"), None),
        P(("seq", "dp"), "head"),
        P("head"),
        P("head"),
        P("head"),
        P("head"),
    )
    return jax.shard_map(
        per_device,
        mesh=mesh,
        in_specs=placed,
        out_specs=P(("grp", "dp"), "seq", "head"),
        check_vma=False,
    )
```

profile of v0, /device:TPU:0, one launch (start us, length us, event | category | flops | bytes accessed | tf_op | source)
XLA Modules:
  0.0 492.6 jit_solution(16244792170298626122)
XLA Ops:
  8.5 1.3 reduce.16
  10.5 6.3 %all-to-all-start.1 = ((s32[1,4,64]{2,0,1:T(1,128)}), s32[1,4,64]{2,0,1:T(1,128)S(1)}, u32[]{:S(2)}, u32[]{:S(2)}) async-start(s32[1,4,64]{2,0,1:T(1,128)} %all_to_all.10), calls=%async_computation.1 | async-start | bytes 4096 | tf_op jit(solution)/shard_map/all_to_all | solution.py:87
  16.9 8.3 %copy.62 = bf16[1,256,4096]{2,0,1:T(2,128)(2,1)} copy(bf16[1,256,4096]{2,1,0:T(8,128)(2,1)} %param.16) | data formatting | bytes 4194304 | tf_op args[0]
  25.7 13.5 %reduce.17 = bf16[256,4096]{1,0:T(8,128)(2,1)S(1)} reduce(bf16[256,1,4096]{2,1,0:T(2,128)(2,1)} %bitcast.140, bf16[]{:T(256)} %broadcast.192), dimensions={1}, to_apply=%bitcast.110.reduce_sub_computation | reduce | bytes 4194306
  39.2 2.8 reshape.243
  42.0 5.2 %all-to-all-start = ((bf16[4,2,131072]{2,1,0:T(2,128)(2,1)}), bf16[4,2,131072]{2,1,0:T(2,128)(2,1)S(1)}, u32[]{:S(2)}, u32[]{:S(2)}) async-start(bf16[4,2,131072]{2,1,0:T(2,128)(2,1)} %reshape.243), calls=%async_computation | async-start | bytes 4194304 | tf_op jit(solution)/shard_map/all_to_all | solution.py:86
  47.7 75.0 %all_gather.27 = bf16[4096,16]{0,1:T(8,128)(2,1)S(1)} all-gather(bf16[256,16]{0,1:T(8,128)(2,1)S(1)} %copy-done.4), channel_id=1, replica_groups=mesh['grp'=1,'seq'=4,'dp'=4,'head'=2] {'seq','dp'}, dimensions={0}, use_global_device_ids=true | all-gather | bytes 139264 | tf_op jit(solution)/shard_map/all_gather | solution.py:39
  123.0 1.6 scatter_custom_fusion
  124.6 3.4 reshape.244
  128.0 4.5 copy.61
  132.5 3.2 gather_fusion
  135.7 2.4 compare_select_fusion.2
  139.0 2.1 convolution_convert_fusion.1
  142.2 142.0 %all-gather.10.cloned.1.call-done = bf16[4096,2048]{1,0:T(8,128)(2,1)} async-done(((bf16[256,2048]{1,0:T(8,128)(2,1)}), bf16[4096,2048]{1,0:T(8,128)(2,1)}) %all-gather.10.cloned.1.call-update) | async-done | bytes 16777232 | tf_op jit(solution)/shard_map/all_gather | solution.py:29
  284.2 8.3 %convolution_convert_fusion = bf16[256,2048]{1,0:T(8,128)(2,1)S(1)} fusion(bf16[256,4096]{1,0:T(8,128)(2,1)S(1)} %copy-done, bf16[4096,2048]{1,0:T(8,128)(2,1)} %all-gather.10.cloned.1.call-done), kind=kOutput, calls=%fused_computation.50 | convolution fusion | flops 4295491584 | bytes 19922944 | tf_op jit(solution)/shard_map/dot_general | solution.py:27
  293.4 87.8 %while.48 = (s32[]{:T(128)}, f32[16,256,128]{1,2,0:T(8,128)}, f32[16,64,128]{2,1,0:T(8,128)}, f32[16,64,128]{2,1,0:T(8,128)}, f32[16,256]{1,0:T(8,128)S(1)}, /*i...) while((s32[]{:T(128)}, f32[16,256,128]{1,2,0:T(8,128)}, ...), condition=%wide.region_6.7_spmd.clone.clone, body=%wide.region_5.6_spmd.clone.clone.sunk | while | flops 151619328 | bytes 937137 | solution.py:109
  295.7 1.3 fusion.84
  301.1 1.3 fusion.84
  306.6 1.3 fusion.84
  312.1 1.3 fusion.84
  317.6 1.3 fusion.84
  323.1 1.3 fusion.84
  361.5 1.3 fusion.84
  383.8 9.2 %all-gather.2 = f32[4,1,16]{2,1,0:T(1,128)S(1)} all-gather(f32[1,1,16]{2,1,0:T(1,128)S(1)} %bitcast.151), channel_id=1, replica_groups=mesh['grp'=1,'seq'=4,'dp'=4,'head'=2] {'seq'}, dimensions={0}, use_global_device_ids=true | all-gather | bytes 320 | tf_op jit(solution)/shard_map/all_gather | solution.py:9
  394.3 1.6 copy.38
  395.9 29.2 %all-gather.14.cloned.1.call-done = f32[64,64,128]{2,1,0:T(8,128)} async-done(((f32[16,64,128]{2,1,0:T(8,128)}), f32[64,64,128]{2,1,0:T(8,128)}) %all-gather.14.cloned.1.call-update) | async-done | bytes 2097168 | tf_op jit(solution)/shard_map/all_gather | solution.py:9
  425.2 4.9 while.47
  430.0 41.1 %all-gather.12.cloned.1.call-done = f32[64,64,128]{2,1,0:T(8,128)} async-done(((f32[16,64,128]{2,1,0:T(8,128)}), f32[64,64,128]{2,1,0:T(8,128)}) %all-gather.12.cloned.1.call-update) | async-done | bytes 2097168 | tf_op jit(solution)/shard_map/all_gather | solution.py:9
  471.1 4.8 while.46
  477.5 2.9 multiply_reduce_fusion
  480.4 1.9 copy.39
  482.4 2.5 psum.7
  (188 shorter events, 100.9 us)
Async XLA Ops:
  6.5 132.5 %all-gather.8.cloned.1.call-start = ((), (), s32[]{:S(2)}) async-start(), calls=%async_computation.2 | async-start | bytes 1114112 | tf_op jit(solution)/shard_map/all_gather | solution.py:34
  7.3 276.9 %all-gather.10.cloned.1.call-start = ((), (), s32[]{:S(2)}) async-start(), calls=%async_computation.3 | async-start | bytes 17825792 | tf_op jit(solution)/shard_map/all_gather | solution.py:29
  10.5 31.5 %all-to-all-start.1 = ((s32[1,4,64]{2,0,1:T(1,128)}), s32[1,4,64]{2,0,1:T(1,128)S(1)}, u32[]{:S(2)}, u32[]{:S(2)}) async-start(s32[1,4,64]{2,0,1:T(1,128)} %all_to_all.10), calls=%async_computation.1 | async-start | bytes 4096 | tf_op jit(solution)/shard_map/all_to_all | solution.py:87
  42.0 5.3 %copy-start.5 = (s32[1,256]{1,0:T(1,128)S(1)}, s32[1,256]{1,0:T(1,128)}, u32[]{:S(2)}) copy-start(s32[1,256]{1,0:T(1,128)} %param.18) | copy-start | bytes 3076
  42.0 5.7 %copy-start.4 = (bf16[256,16]{0,1:T(8,128)(2,1)S(1)}, bf16[256,16]{0,1:T(8,128)(2,1)}, u32[]{:S(2)}) copy-start(bf16[256,16]{0,1:T(8,128)(2,1)} %param.21) | copy-start | bytes 24580
  42.0 80.8 %copy-start.8 = (f32[16]{0:T(128)S(1)}, f32[16]{0:T(128)}, u32[]{:S(2)}) copy-start(f32[16]{0:T(128)} %param.23) | copy-start | bytes 196
  42.0 82.6 %all-to-all-start = ((bf16[4,2,131072]{2,1,0:T(2,128)(2,1)}), bf16[4,2,131072]{2,1,0:T(2,128)(2,1)S(1)}, u32[]{:S(2)}, u32[]{:S(2)}) async-start(bf16[4,2,131072]{2,1,0:T(2,128)(2,1)} %reshape.243), calls=%async_computation | async-start | bytes 4194304 | tf_op jit(solution)/shard_map/all_to_all | solution.py:86
  47.3 377.9 %all-gather.14.cloned.1.call-start = ((), (), s32[]{:S(2)}) async-start(), calls=%async_computation.5 | async-start | bytes 2621440 | tf_op jit(solution)/shard_map/all_gather | solution.py:9
  132.5 3.2 copy-start.6
  135.7 3.3 copy-start
  292.4 1.0 copy-start.2
  381.2 89.9 %all-gather.12.cloned.1.call-start = ((), (), s32[]{:S(2)}) async-start(), calls=%async_computation.4 | async-start | bytes 2621440 | tf_op jit(solution)/shard_map/all_gather | solution.py:9
  475.9 1.6 copy-start.1
  475.9 1.6 copy-start.7
  480.4 4.4 copy-start.3
Sparse Core Ops, SparseCore 0:
  10.1 61.7 all-gather.7
  74.7 209.4 all-gather.9
  381.3 43.8 all-gather.13
  426.6 44.4 all-gather.11
where the time goes:
time: 494 us; the launch traced here: 493 us
  waiting for transfers between devices  214 us (43%)
  blocking collectives  86.6 us (18%)
  matrix products  65.4 us (13%)
  local copies, waits for them, and re-layouts  52.1 us (11%)
  other arithmetic  48.2 us (10%)
  between operations  14 us (3%)
  starting transfers between devices  11.7 us (2%)
    all_gather x1, waiting for transfers between devices, project_rows(): lax.all_gather(feature_weight, ('seq', 'dp'), axis=0, tiled=True)  142 us
    all_gather x1, blocking collectives, project_rows(): lax.all_gather(step_weight, ('seq', 'dp'), axis=0, tiled=True)  75 us
    all_gather x2, waiting for transfers between devices, entering(): everything = jax.tree.map(lambda part: lax.all_gather(part, axis), value)  70.3 us
    unnamed x26, local copies, waits for them, and re-layouts  22.6 us
    mul x16, other arithmetic, head_terms(): begin_weight = jnp.exp(cum_head) * (doc_index == 0) * step_head  20.6 us
    dot_general x16, matrix products, head_terms(): y_local = jnp.dot(mixing, x_float, precision=lax.Precision.HIGHEST)  17.7 us
    dot_general x16, matrix products, head_terms(): jnp.dot((b_float * end_weight[:, None]).T, x_float, precision=lax.Precisi...  15.1 us
    dot_general x16, matrix products, head_terms(): jnp.dot((b_float * begin_weight[:, None]).T, x_float, precision=lax.Preci...  15 us
  transfers between devices with their start and end apart: 6, of which 3 were waited for; matrix products, arithmetic and copies ran while one was open for 11% of the time, Pallas kernels for 0%

commit v1 on v0

v1 whole, which is shorter than its diff:
```python
import jax
import jax.numpy as jnp
from jax import lax
from jax.sharding import PartitionSpec as P

HIGH = lax.Precision.HIGHEST


def carried(gains, states, here, reverse):
    count = gains.shape[0]
    k = jnp.arange(count)[:, None]
    u = jnp.arange(count)[None, :]
    if reverse:
        source = k > here
        between = (u > here) & (u < k)
    else:
        source = k < here
        between = (u > k) & (u < here)
    factors = jnp.where(between[:, :, None], gains[None, :, :], 1.0)
    weight = jnp.prod(factors, axis=1) * source.astype(jnp.float32)
    return jnp.sum(weight[:, :, None, None] * states, axis=0)


def per_device(
    tokens_in,
    positions,
    doc_start,
    feature_weight,
    state_weight,
    step_weight,
    step_bias,
    decay_log,
    skip_gain,
    norm_gain,
):
    row_count = tokens_in.shape[1]
    width = tokens_in.shape[2]
    shards = lax.axis_size("seq")
    here = lax.axis_index("seq")
    slot = row_count // shards
    rows = tokens_in[0].reshape(shards, slot, width)
    moved_rows = lax.all_to_all(rows, "seq", 0, 0, tiled=True).reshape(row_count, width)
    moved_positions = lax.all_to_all(
        positions[0].reshape(shards, slot), "seq", 0, 0, tiled=True
    ).reshape(row_count)
    offsets = moved_positions - here * row_count
    inverse = jnp.zeros((row_count,), jnp.int32).at[offsets].set(
        jnp.arange(row_count, dtype=jnp.int32)
    )
    features = moved_rows[inverse]

    head_count = step_bias.shape[0]
    feat_cols = feature_weight.shape[1]
    head_size = feat_cols // head_count
    state_size = state_weight.shape[1] // 2
    weights = jnp.concatenate([feature_weight, state_weight, step_weight], axis=1)
    gathered = lax.all_gather(weights, ("seq", "dp"), axis=0, tiled=True)
    proj = jnp.dot(features, gathered, preferred_element_type=jnp.float32).astype(jnp.bfloat16)
    x_proj = proj[:, :feat_cols]
    bc_proj = proj[:, feat_cols : feat_cols + 2 * state_size]
    step_raw = proj[:, feat_cols + 2 * state_size :]

    b_float = bc_proj[:, :state_size].astype(jnp.float32)
    c_float = bc_proj[:, state_size:].astype(jnp.float32)
    step_size = jax.nn.softplus(step_raw.astype(jnp.float32) + step_bias[None, :])
    log_decay = -jnp.exp(decay_log)[None, :] * step_size
    cum_decay = jnp.cumsum(log_decay, axis=0)
    doc_index = jnp.cumsum(doc_start[0], axis=0)
    scores = jnp.dot(
        bc_proj[:, state_size:], bc_proj[:, :state_size].T, preferred_element_type=jnp.float32
    )
    places = jnp.arange(row_count, dtype=jnp.int32)
    same_doc = (
        (doc_index[:, None] == doc_index[None, :]) & (places[:, None] != places[None, :])
    ).astype(jnp.float32)
    cum_t = cum_decay.T
    step_t = step_size.T
    decay = jnp.exp(-jnp.abs(cum_t[:, :, None] - cum_t[:, None, :])) * same_doc[None]
    mixing = scores[None] * decay * step_t[:, None, :]
    x_heads = x_proj.reshape(row_count, head_count, head_size).astype(jnp.float32)
    y_local = jnp.einsum("hts,shp->thp", mixing, x_heads, precision=HIGH)

    last_doc = (doc_index == doc_index[-1]).astype(jnp.float32)
    first_doc = (doc_index == 0).astype(jnp.float32)
    end_weight = jnp.exp(cum_decay[-1][None, :] - cum_decay) * last_doc[:, None] * step_size
    begin_weight = jnp.exp(cum_decay) * first_doc[:, None] * step_size
    state_end = jnp.einsum("tn,th,thp->hnp", b_float, end_weight, x_heads, precision=HIGH)
    state_begin = jnp.einsum("tn,th,thp->hnp", b_float, begin_weight, x_heads, precision=HIGH)
    carry_gain = jnp.exp(cum_decay[-1]) * (doc_index[-1] == 0)

    state_rows = 2 * head_count * state_size
    gain_rows = jnp.zeros((8, head_size), jnp.float32).at[0, :head_count].set(carry_gain)
    packed = jnp.concatenate(
        [state_end.reshape(-1, head_size), state_begin.reshape(-1, head_size), gain_rows]
    )
    every = lax.all_gather(packed, "seq", axis=0, tiled=True).reshape(shards, -1, head_size)
    gains = every[:, state_rows, :head_count]
    state_shape = (shards,) + state_end.shape
    ends = every[:, : state_rows // 2].reshape(state_shape)
    begins = every[:, state_rows // 2 : state_rows].reshape(state_shape)
    prefix = carried(gains, ends, here, False)
    suffix = carried(gains, begins, here, True)

    left_gate = jnp.exp(cum_decay) * first_doc[:, None]
    right_gate = jnp.exp(cum_decay[-1][None, :] - cum_decay) * last_doc[:, None]
    from_left = jnp.einsum("tn,hnp->thp", c_float, prefix, precision=HIGH)
    from_right = jnp.einsum("tn,hnp->thp", c_float, suffix, precision=HIGH)
    mixer = (
        y_local
        + left_gate[:, :, None] * from_left
        + right_gate[:, :, None] * from_right
        + skip_gain[None, :, None] * x_heads
    )
    mixer_rows = mixer.reshape(row_count, head_count * head_size)
    square_sum = lax.psum(jnp.sum(mixer_rows * mixer_rows, axis=1), "head")
    full_width = mixer_rows.shape[1] * lax.axis_size("head")
    inv_scale = lax.rsqrt(square_sum / full_width + 1e-05)
    return (mixer_rows * inv_scale[:, None] * norm_gain[None, :]).astype(jnp.bfloat16)[None]


def solution(mesh):
    placed = (
        P(("grp", "dp"), "seq", None),
        P(("grp", "dp"), "seq"),
        P(("grp", "dp"), "seq"),
        P(("seq", "dp"), "head"),
        P(("seq", "dp"), None),
        P(("seq", "dp"), "head"),
        P("head"),
        P("head"),
        P("head"),
        P("head"),
    )
    return jax.shard_map(
        per_device,
        mesh=mesh,
        in_specs=placed,
        out_specs=P(("grp", "dp"), "seq", "head"),
        check_vma=False,
    )
```

time: 494 us -> 380 us (0.77)
  waiting for transfers between devices: 214 us -> 301 us
  blocking collectives: 86.6 us -> 14.2 us
  matrix products: 65.4 us -> 23.6 us
  local copies, waits for them, and re-layouts: 52.1 us -> 10.7 us
  other arithmetic: 48.2 us -> 11.7 us
  starting transfers between devices: 11.7 us -> 3.79 us
    all_to_all x2 -> x1, waiting for transfers between devices: 0.01 us -> 96 us  [per_device(): lax.all_to_all(rows, 'seq', 0, 0, tiled=True).reshape(row_count, width)]
    all_gather x2 -> x0, blocking collectives: 84.1 us -> none  [the longest x1 75 us: project_rows(): lax.all_gather(step_weight, ('seq', 'dp'), axis=0, tiled=True)]
    dot_general x53 -> x6, matrix products: 64.5 us -> 23.4 us  [the longest x1 11.9 us: per_device(): jnp.dot(features, gathered, preferred_element_type=jnp.float32)]
    unnamed x26 -> x17, local copies, waits for them, and re-layouts: 22.6 us -> 2.04 us
    mul x17 -> x3, other arithmetic: 20.7 us -> 0.24 us  [the longest x2 0.14 us: carried(): weight = jnp.prod(factors, axis=1) * source.astype(jnp.float32)]
    slice x34 -> x3, local copies, waits for them, and re-layouts: 19.8 us -> 1.37 us  [the longest x1 0.72 us: per_device(): gains = every[:, state_rows, :head_count]]
    unnamed x4 -> x1, other arithmetic: 14.8 us -> 0.66 us
    all_to_all x0 -> x1, blocking collectives: none -> 11.7 us  [per_device(): lax.all_to_all(positions[0].reshape(shards, slot), 'seq', 0, 0, tiled=True)]
  transfers between devices with their start and end apart: 6 -> 3, of which waited for: 3 -> 3; matrix products, arithmetic and copies ran while one was open for 11% -> 3% of each run, Pallas kernels for 0% -> 0%
where the time goes in v1:
time: 380 us
  waiting for transfers between devices  301 us (79%)
  matrix products  23.6 us (6%)
  between operations  14.3 us (4%)
  blocking collectives  14.2 us (4%)
  other arithmetic  11.7 us (3%)
  local copies, waits for them, and re-layouts  10.7 us (3%)
    all_gather x1, waiting for transfers between devices, per_device(): gathered = lax.all_gather(weights, ('seq', 'dp'), axis=0, tiled=True)  130 us
    all_to_all x1, waiting for transfers between devices, per_device(): lax.all_to_all(rows, 'seq', 0, 0, tiled=True).reshape(row_count, width)  96 us
    all_gather x1, waiting for transfers between devices, per_device(): lax.all_gather(packed, 'seq', axis=0, tiled=True)  75.6 us
    dot_general x1, matrix products, per_device(): jnp.dot(features, gathered, preferred_element_type=jnp.float32)  11.9 us
    all_to_all x1, blocking collectives, per_device(): lax.all_to_all(positions[0].reshape(shards, slot), 'seq', 0, 0, tiled=True)  11.7 us
  transfers between devices with their start and end apart: 3, of which 3 were waited for; matrix products, arithmetic and copies ran while one was open for 3% of the time, Pallas kernels for 0%

profile of v1, /device:TPU:0, one launch (start us, length us, event | category | flops | bytes accessed | tf_op | source)
XLA Modules:
  0.0 379.5 jit_solution(17358106147090608229)
XLA Ops:
  6.5 0.8 copy.32
  7.4 2.4 pad_maximum_fusion
  9.8 0.5 broadcast.256
  10.3 0.7 reduce.18
  11.0 11.7 %all_to_all.14 = s32[4,1,64]{2,1,0:T(1,128)S(1)} all-to-all(s32[4,1,64]{2,1,0:T(1,128)S(1)} %all_to_all.10), channel_id=1, replica_groups=mesh['grp'=1,'seq'=4,'dp'=4,'head'=2] {'seq'}, dimensions={0} | all-to-all | bytes 2048 | tf_op jit(solution)/shard_map/all_to_all | solution.py:43
  22.7 3.7 all-to-all-start
  26.5 0.3 reduce-window.19
  27.0 0.1 slice_reduce_fusion.2
  27.2 0.6 slice.73
  28.4 0.7 compare_convert_fusion
  29.2 1.4 scatter_custom_fusion
  30.6 96.0 %all-to-all-done = bf16[4,64,4096]{2,1,0:T(8,128)(2,1)S(1)} async-done(((bf16[4,64,4096]{2,1,0:T(8,128)(2,1)}), bf16[4,64,4096]{2,1,0:T(8,128)(2,1)S(1)}, u32[]{:S(2)}, u32[]{:S(2)}) %all-to-all-start) | async-done | bytes 2097184 | tf_op jit(solution)/shard_map/all_to_all | solution.py:42
  126.6 3.1 gather_fusion
  129.8 129.7 %all-gather.3.cloned.1.call-done = bf16[4096,2192]{1,0:T(8,128)(2,1)} async-done(((bf16[256,2192]{1,0:T(8,128)(2,1)}), bf16[4096,2192]{1,0:T(8,128)(2,1)}) %all-gather.3.cloned.1.call-update) | async-done | bytes 17956880 | tf_op jit(solution)/shard_map/all_gather | solution.py:57
  259.5 11.9 %convolution_convert_fusion = bf16[256,2192]{0,1:T(8,128)(2,1)S(1)} fusion(bf16[256,4096]{1,0:T(8,128)(2,1)} %gather_fusion, bf16[4096,2192]{1,0:T(8,128)(2,1)} %all-gather.3.cloned.1.call-done), kind=kOutput, calls=%fused_computation.10 | convolution fusion | flops 4597518336 | bytes 21176320 | tf_op jit(solution)/shard_map/dot_general | solution.py:58
  271.5 0.6 copy-done.2
  272.1 0.6 reduce-window.15
  272.7 0.2 slice_reduce_fusion
  273.0 0.2 slice_reduce_fusion.1
  273.3 1.3 fusion.8
  274.6 1.3 fusion.9
  276.0 1.1 select_maximum_fusion
  277.3 0.2 fusion.30
  277.5 3.4 fusion
  280.9 75.6 %all-gather.5.cloned.1.call-done = f32[8224,128]{1,0:T(8,128)} async-done(((f32[2056,128]{1,0:T(8,128)}), f32[8224,128]{1,0:T(8,128)}) %all-gather.5.cloned.1.call-update) | async-done | bytes 4210704 | tf_op jit(solution)/shard_map/all_gather | solution.py:96
  356.5 0.7 slice.85
  357.7 3.8 %fusion.11 = (f32[1024,128]{1,0:T(8,128)S(1)}, f32[1024,128]{1,0:T(8,128)S(1)}) fusion(f32[4,2056,128]{2,1,0:T(8,128)} %bitcast.80, f32[4,1024]{1,0:T(4,128)S(1)} %mul.209, f32[4,1024]{1,0:T(4,128)S(1)} %mul.201), kind=kLoop, calls=%fused_computation.18 | loop fusion | flops 1835008 | bytes 5275648 | tf_op jit(solution)/shard_map/reduce_sum | solution.py:21
  361.6 1.8 fusion.24
  363.4 3.7 multiply_reduce_fusion
  367.1 1.9 copy.38
  369.0 2.5 psum.7
  371.5 1.2 multiply_convert_fusion
  (48 shorter events, 1.7 us)
Async XLA Ops:
  6.5 3.7 copy-start.3
  6.5 253.0 %all-gather.3.cloned.1.call-start = ((), (), s32[]{:S(2)}) async-start(), calls=%async_computation.2 | async-start | bytes 20054016 | tf_op jit(solution)/shard_map/all_gather | solution.py:57
  22.7 3.8 %copy-start.4 = (s32[1,256]{1,0:T(1,128)S(1)}, s32[1,256]{1,0:T(1,128)}, u32[]{:S(2)}) copy-start(s32[1,256]{1,0:T(1,128)} %param.14) | copy-start | bytes 3076
  22.7 5.7 %copy-start.6 = (f32[16]{0:T(128)S(1)}, f32[16]{0:T(128)}, u32[]{:S(2)}) copy-start(f32[16]{0:T(128)} %param.19) | copy-start | bytes 196
  22.7 103.9 %all-to-all-start = ((bf16[4,64,4096]{2,1,0:T(8,128)(2,1)}), bf16[4,64,4096]{2,1,0:T(8,128)(2,1)S(1)}, u32[]{:S(2)}, u32[]{:S(2)}) async-start(bf16[4,64,4096]{2,1,0:T(8,128)(2,1)} %bitcast.84), calls=%async_computation | async-start | bytes 4194304 | tf_op jit(solution)/shard_map/all_to_all | solution.py:42
  26.5 330.0 %all-gather.5.cloned.1.call-start = ((), (), s32[]{:S(2)}) async-start(), calls=%async_computation.3 | async-start | bytes 5263360 | tf_op jit(solution)/shard_map/all_gather | solution.py:96
  271.4 5.9 %copy-start = (bf16[256,2192]{0,1:T(8,128)(2,1)}, bf16[256,2192]{0,1:T(8,128)(2,1)S(1)}, u32[]{:S(2)}) copy-start(bf16[256,2192]{0,1:T(8,128)(2,1)S(1)} %convolution_convert_fusion) | copy-start | bytes 3366916
  271.4 0.7 copy-start.2
  361.6 1.8 copy-start.5
  367.1 4.4 %copy-start.1 = (f32[2048]{0:T(1024)S(1)}, f32[2048]{0:T(1024)}, u32[]{:S(2)}) copy-start(f32[2048]{0:T(1024)} %param.21) | copy-start | bytes 24580
Sparse Core Ops, SparseCore 0:
  10.1 249.3 all-gather.2
  277.2 79.1 all-gather.4

commit v2 on v1

--- a/solution.py
+++ b/solution.py
@@ -6,19 +6,36 @@
 HIGH = lax.Precision.HIGHEST
 
 
-def carried(gains, states, here, reverse):
-    count = gains.shape[0]
-    k = jnp.arange(count)[:, None]
-    u = jnp.arange(count)[None, :]
-    if reverse:
-        source = k > here
-        between = (u > here) & (u < k)
-    else:
-        source = k < here
-        between = (u > k) & (u < here)
-    factors = jnp.where(between[:, :, None], gains[None, :, :], 1.0)
-    weight = jnp.prod(factors, axis=1) * source.astype(jnp.float32)
-    return jnp.sum(weight[:, :, None, None] * states, axis=0)
+def carried(gain, state, axis, reverse):
+    count = lax.axis_size(axis)
+    here = lax.axis_index(axis)
+    rows = state.shape[0] * state.shape[1]
+    pad = jnp.zeros((8, state.shape[2]), state.dtype).at[0, : gain.shape[0]].set(gain)
+    value = jnp.concatenate([state.reshape(rows, -1), pad])
+
+    def shift(x, step):
+        if reverse:
+            pairs = [(j, j - step) for j in range(step, count)]
+            reached = here < count - step
+        else:
+            pairs = [(j, j + step) for j in range(count - step)]
+            reached = here >= step
+        return lax.ppermute(x, axis, pairs), reached
+
+    value, reached = shift(value, 1)
+    value = value.at[rows].set(jnp.where(reached, value[rows], 1.0))
+    step = 1
+    while step < count:
+        earlier, reached = shift(value, step)
+        g_early = jnp.where(reached, earlier[rows, : gain.shape[0]], 1.0)
+        g_late = value[rows, : gain.shape[0]]
+        late = value[:rows].reshape(state.shape)
+        merged = g_late[:, None, None] * earlier[:rows].reshape(state.shape) + late
+        value = jnp.concatenate(
+            [merged.reshape(rows, -1), value[rows:].at[0, : gain.shape[0]].set(g_early * g_late)]
+        )
+        step *= 2
+    return value[:rows].reshape(state.shape)
 
 
 def per_device(
@@ -88,18 +105,8 @@
     state_begin = jnp.einsum("tn,th,thp->hnp", b_float, begin_weight, x_heads, precision=HIGH)
     carry_gain = jnp.exp(cum_decay[-1]) * (doc_index[-1] == 0)
 
-    state_rows = 2 * head_count * state_size
-    gain_rows = jnp.zeros((8, head_size), jnp.float32).at[0, :head_count].set(carry_gain)
-    packed = jnp.concatenate(
-        [state_end.reshape(-1, head_size), state_begin.reshape(-1, head_size), gain_rows]
-    )
-    every = lax.all_gather(packed, "seq", axis=0, tiled=True).reshape(shards, -1, head_size)
-    gains = every[:, state_rows, :head_count]
-    state_shape = (shards,) + state_end.shape
-    ends = every[:, : state_rows // 2].reshape(state_shape)
-    begins = every[:, state_rows // 2 : state_rows].reshape(state_shape)
-    prefix = carried(gains, ends, here, False)
-    suffix = carried(gains, begins, here, True)
+    prefix = carried(carry_gain, state_end, "seq", False)
+    suffix = carried(carry_gain, state_begin, "seq", True)
 
     left_gate = jnp.exp(cum_decay) * first_doc[:, None]
     right_gate = jnp.exp(cum_decay[-1][None, :] - cum_decay) * last_doc[:, None]

time: 380 us -> 361 us (0.950)
  waiting for transfers between devices: 301 us -> 258 us
  starting transfers between devices: 3.79 us -> 21.5 us
  other arithmetic: 11.7 us -> 16.2 us
    all_gather x1 -> x0, waiting for transfers between devices: 75.6 us -> none  [per_device(): lax.all_gather(packed, 'seq', axis=0, tiled=True)]
    ppermute x0 -> x6, waiting for transfers between devices: none -> 31.7 us  [shift(): return (lax.ppermute(x, axis, pairs), reached)]
    ppermute x0 -> x6, starting transfers between devices: none -> 17.8 us  [shift(): return (lax.ppermute(x, axis, pairs), reached)]
    reduce_sum x1 -> x0, other arithmetic: 3.8 us -> none  [carried(): return jnp.sum(weight[:, :, None, None] * states, axis=0)]
  transfers between devices with their start and end apart: 3 -> 8, of which waited for: 3 -> 7; matrix products, arithmetic and copies ran while one was open for 3% -> 7% of each run, Pallas kernels for 0% -> 0%
where the time goes in v2:
time: 361 us; the launch traced here: 360 us
  waiting for transfers between devices  258 us (71%)
  matrix products  23.2 us (6%)
  starting transfers between devices  21.5 us (6%)
  other arithmetic  16.2 us (4%)
  between operations  14.4 us (4%)
  blocking collectives  14.2 us (4%)
  local copies, waits for them, and re-layouts  13.2 us (4%)
    all_gather x1, waiting for transfers between devices, per_device(): gathered = lax.all_gather(weights, ('seq', 'dp'), axis=0, tiled=True)  130 us
    all_to_all x1, waiting for transfers between devices, per_device(): lax.all_to_all(rows, 'seq', 0, 0, tiled=True).reshape(row_count, width)  96 us
    ppermute x6, waiting for transfers between devices, shift(): return (lax.ppermute(x, axis, pairs), reached)  31.7 us
    ppermute x6, starting transfers between devices, shift(): return (lax.ppermute(x, axis, pairs), reached)  17.8 us
    dot_general x1, matrix products, per_device(): jnp.dot(features, gathered, preferred_element_type=jnp.float32)  11.9 us
    all_to_all x1, blocking collectives, per_device(): lax.all_to_all(positions[0].reshape(shards, slot), 'seq', 0, 0, tiled=True)  11.7 us
  transfers between devices with their start and end apart: 8, of which 7 were waited for; matrix products, arithmetic and copies ran while one was open for 7% of the time, Pallas kernels for 0%

profile of v2, /device:TPU:0, one launch (start us, length us, event | category | flops | bytes accessed | tf_op | source)
XLA Modules:
  0.0 360.2 jit_solution(5522537520040137037)
XLA Ops:
  7.4 2.4 pad_maximum_fusion
  11.0 11.7 %all_to_all.14 = s32[4,1,64]{2,1,0:T(1,128)S(1)} all-to-all(s32[4,1,64]{2,1,0:T(1,128)S(1)} %all_to_all.10), channel_id=1, replica_groups=mesh['grp'=1,'seq'=4,'dp'=4,'head'=2] {'seq'}, dimensions={0} | all-to-all | bytes 2048 | tf_op jit(solution)/shard_map/all_to_all | solution.py:60
  22.7 3.7 %all-to-all-start = ((bf16[4,64,4096]{2,1,0:T(8,128)(2,1)}), bf16[4,64,4096]{2,1,0:T(8,128)(2,1)S(1)}, u32[]{:S(2)}, u32[]{:S(2)}) async-start(bf16[4,64,4096]{2,1,0:T(8,128)(2,1)} %bitcast.96), calls=%async_computation | async-start | bytes 4194304 | tf_op jit(solution)/shard_map/all_to_all | solution.py:59
  29.2 1.4 scatter_custom_fusion
  30.6 96.0 %all-to-all-done = bf16[4,64,4096]{2,1,0:T(8,128)(2,1)S(1)} async-done(((bf16[4,64,4096]{2,1,0:T(8,128)(2,1)}), bf16[4,64,4096]{2,1,0:T(8,128)(2,1)S(1)}, u32[]{:S(2)}, u32[]{:S(2)}) %all-to-all-start) | async-done | bytes 2097184 | tf_op jit(solution)/shard_map/all_to_all | solution.py:59
  126.6 3.1 gather_fusion
  129.8 129.7 %all-gather.2.cloned.1.call-done = bf16[4096,2192]{1,0:T(8,128)(2,1)} async-done(((bf16[256,2192]{1,0:T(8,128)(2,1)}), bf16[4096,2192]{1,0:T(8,128)(2,1)}) %all-gather.2.cloned.1.call-update) | async-done | bytes 17956880 | tf_op jit(solution)/shard_map/all_gather | solution.py:74
  259.5 11.9 %convolution_convert_fusion = bf16[256,2192]{0,1:T(8,128)(2,1)S(1)} fusion(bf16[256,4096]{1,0:T(8,128)(2,1)} %gather_fusion, bf16[4096,2192]{1,0:T(8,128)(2,1)} %all-gather.2.cloned.1.call-done), kind=kOutput, calls=%fused_computation.10 | convolution fusion | flops 4597518336 | bytes 21176320 | tf_op jit(solution)/shard_map/dot_general | solution.py:75
  273.3 1.3 fusion.8
  274.6 1.3 fusion.9
  276.0 1.0 fusion.20
  277.0 1.6 collective-permute-start
  278.7 1.3 collective-permute-start.3
  280.2 9.2 %collective-permute-done = f32[1032,128]{1,0:T(8,128)S(1)} collective-permute-done((f32[1032,128]{1,0:T(8,128)}, f32[1032,128]{1,0:T(8,128)S(1)}, u32[]{:S(2)}, u32[]{:S(2)}) %collective-permute-start) | collective-permute-done | bytes 528416 | tf_op jit(solution)/shard_map/ppermute | solution.py:23
  289.5 5.1 %collective-permute-start.1 = (f32[1032,128]{1,0:T(8,128)S(1)}, f32[1032,128]{1,0:T(8,128)}, u32[]{:S(2)}, u32[]{:S(2)}) collective-permute-start(f32[1032,128]{1,0:T(8,128)S(1)} %scatter.26), channel_id=1, source_target_pairs={{0,8},{8,16},{16,24},{1,9},{9,17},{17,25},{2,10},{10,18},{18,26},{... | collective-permute-start | bytes 1585160 | tf_op jit(solution)/shard_map/ppermute | solution.py:23
  294.6 4.6 %fusion = f32[16,128,256]{2,1,0:T(8,128)} fusion(bf16[256,16,128]{0,2,1:T(8,128)(2,1)S(1)} %bitcast.88, f32[16,256]{1,0:T(8,128)S(1)} %get-tuple-element.81, f32[256,256]{1,0:T(8,128)S(1)} %fusion.35, f32[16,256]{1,0:T(8,128)S(1)} %get-tuple-element.91, f32[256,256]{1,0:T(8,128)S(1)} %fusion.42), kind=kOutput, calls=%fused_computation.2 | convolution fusion | flops 1616904192 | bytes 3702784 | tf_op jit(solution)/shard_map/hts,shp->thp/dot_general | solution.py:98
  299.9 1.3 scatter.30
  301.2 1.5 collective-permute-start.4
  304.5 1.4 multiply_add_fusion.1
  305.9 0.8 pad_maximum_fusion.1
  306.8 7.1 %collective-permute-start.2 = (f32[1032,128]{1,0:T(8,128)}, f32[1032,128]{1,0:T(8,128)}, u32[]{:S(2)}, u32[]{:S(2)}) collective-permute-start(f32[1032,128]{1,0:T(8,128)} %pad_maximum_fusion.1), channel_id=1, source_target_pairs={{0,16},{8,24},{1,17},{9,25},{2,18},{10,26},{3,19},{11,27},{4,20},{... | collective-permute-start | bytes 1585160 | tf_op jit(solution)/shard_map/ppermute | solution.py:23
  313.9 1.5 collective-permute-done.4
  316.3 1.4 multiply_add_fusion
  317.8 1.3 collective-permute-start.5
  320.4 2.0 collective-permute-done.2
  322.5 1.1 slice.216
  323.6 1.3 fusion.25
  324.9 18.7 %collective-permute-done.5 = f32[1032,128]{1,0:T(8,128)S(1)} collective-permute-done((f32[1032,128]{1,0:T(8,128)S(1)}, f32[1032,128]{1,0:T(8,128)S(1)}, u32[]{:S(2)}, u32[]{:S(2)}) %collective-permute-start.5) | collective-permute-done | bytes 528416 | tf_op jit(solution)/shard_map/ppermute | solution.py:23
  343.6 2.6 multiply_reduce_fusion
  346.2 1.9 copy.34
  348.1 2.4 psum.7
  350.6 2.8 multiply_convert_fusion
  (70 shorter events, 11.3 us)
Async XLA Ops:
  6.5 3.7 %copy-start.5 = (s32[1,256]{1,0:T(1,128)S(1)}, s32[1,256]{1,0:T(1,128)}, u32[]{:S(2)}) copy-start(s32[1,256]{1,0:T(1,128)} %param.23) | copy-start | bytes 3076
  6.5 253.0 %all-gather.2.cloned.1.call-start = ((), (), s32[]{:S(2)}) async-start(), calls=%async_computation.2 | async-start | bytes 20054016 | tf_op jit(solution)/shard_map/all_gather | solution.py:74
  22.7 3.8 %copy-start.6 = (s32[1,256]{1,0:T(1,128)S(1)}, s32[1,256]{1,0:T(1,128)}, u32[]{:S(2)}) copy-start(s32[1,256]{1,0:T(1,128)} %param.24) | copy-start | bytes 3076
  22.7 5.6 %copy-start.8 = (f32[16]{0:T(128)S(1)}, f32[16]{0:T(128)}, u32[]{:S(2)}) copy-start(f32[16]{0:T(128)} %param.29) | copy-start | bytes 196
  22.7 103.9 %all-to-all-start = ((bf16[4,64,4096]{2,1,0:T(8,128)(2,1)}), bf16[4,64,4096]{2,1,0:T(8,128)(2,1)S(1)}, u32[]{:S(2)}, u32[]{:S(2)}) async-start(bf16[4,64,4096]{2,1,0:T(8,128)(2,1)} %bitcast.96), calls=%async_computation | async-start | bytes 4194304 | tf_op jit(solution)/shard_map/all_to_all | solution.py:59
  271.4 52.2 %copy-start.1 = (bf16[256,2192]{0,1:T(8,128)(2,1)}, bf16[256,2192]{0,1:T(8,128)(2,1)S(1)}, u32[]{:S(2)}) copy-start(bf16[256,2192]{0,1:T(8,128)(2,1)S(1)} %convolution_convert_fusion) | copy-start | bytes 3366916
  271.4 0.7 copy-start.4
  277.0 12.4 %collective-permute-start = (f32[1032,128]{1,0:T(8,128)}, f32[1032,128]{1,0:T(8,128)S(1)}, u32[]{:S(2)}, u32[]{:S(2)}) collective-permute-start(f32[1032,128]{1,0:T(8,128)} %get-tuple-element.95), channel_id=1, source_target_pairs={{0,8},{8,16},{16,24},{1,9},{9,17},{17,25},{2,10},{10,18},{18,26},{... | collective-permute-start | bytes 1585160 | tf_op jit(solution)/shard_map/ppermute | solution.py:23
  278.7 20.5 %collective-permute-start.3 = (f32[1032,128]{1,0:T(8,128)}, f32[1032,128]{1,0:T(8,128)}, u32[]{:S(2)}, u32[]{:S(2)}) collective-permute-start(f32[1032,128]{1,0:T(8,128)} %get-tuple-element.94), channel_id=1, source_target_pairs={{8,0},{16,8},{24,16},{9,1},{17,9},{25,17},{10,2},{18,10},{26,18},{... | collective-permute-start | bytes 1585160 | tf_op jit(solution)/shard_map/ppermute | solution.py:23
  289.5 9.7 %copy-start.2 = (f32[1032,128]{1,0:T(8,128)}, f32[1032,128]{1,0:T(8,128)S(1)}, u32[]{:S(2)}) copy-start(f32[1032,128]{1,0:T(8,128)S(1)} %scatter.26) | copy-start | bytes 1585156
  289.5 14.1 %collective-permute-start.1 = (f32[1032,128]{1,0:T(8,128)S(1)}, f32[1032,128]{1,0:T(8,128)}, u32[]{:S(2)}, u32[]{:S(2)}) collective-permute-start(f32[1032,128]{1,0:T(8,128)S(1)} %scatter.26), channel_id=1, source_target_pairs={{0,8},{8,16},{16,24},{1,9},{9,17},{17,25},{2,10},{10,18},{18,26},{... | collective-permute-start | bytes 1585160 | tf_op jit(solution)/shard_map/ppermute | solution.py:23
  301.2 14.2 %collective-permute-start.4 = (f32[1032,128]{1,0:T(8,128)}, f32[1032,128]{1,0:T(8,128)}, u32[]{:S(2)}, u32[]{:S(2)}) collective-permute-start(f32[1032,128]{1,0:T(8,128)} %scatter.30), channel_id=1, source_target_pairs={{8,0},{16,8},{24,16},{9,1},{17,9},{25,17},{10,2},{18,10},{26,18},{... | collective-permute-start | bytes 1585160 | tf_op jit(solution)/shard_map/ppermute | solution.py:23
  306.8 15.7 %collective-permute-start.2 = (f32[1032,128]{1,0:T(8,128)}, f32[1032,128]{1,0:T(8,128)}, u32[]{:S(2)}, u32[]{:S(2)}) collective-permute-start(f32[1032,128]{1,0:T(8,128)} %pad_maximum_fusion.1), channel_id=1, source_target_pairs={{0,16},{8,24},{1,17},{9,25},{2,18},{10,26},{3,19},{11,27},{4,20},{... | collective-permute-start | bytes 1585160 | tf_op jit(solution)/shard_map/ppermute | solution.py:23
  317.8 25.8 %collective-permute-start.5 = (f32[1032,128]{1,0:T(8,128)S(1)}, f32[1032,128]{1,0:T(8,128)S(1)}, u32[]{:S(2)}, u32[]{:S(2)}) collective-permute-start(f32[1032,128]{1,0:T(8,128)S(1)} %pad_maximum_fusion.2), channel_id=1, source_target_pairs={{16,0},{24,8},{17,1},{25,9},{18,2},{26,10},{19,3},{27,11},{20,4},{... | collective-permute-start | bytes 1585160 | tf_op jit(solution)/shard_map/ppermute | solution.py:23
  323.6 20.0 %copy-start = (f32[16,128,256]{2,1,0:T(8,128)S(1)}, f32[16,128,256]{2,1,0:T(8,128)}, u32[]{:S(2)}) copy-start(f32[16,128,256]{2,1,0:T(8,128)} %fusion) | copy-start | bytes 6291460
  323.6 20.0 %copy-start.7 = (f32[16]{0:T(128)S(1)}, f32[16]{0:T(128)}, u32[]{:S(2)}) copy-start(f32[16]{0:T(128)} %param.30) | copy-start | bytes 196
  346.2 4.3 %copy-start.3 = (f32[2048]{0:T(1024)S(1)}, f32[2048]{0:T(1024)}, u32[]{:S(2)}) copy-start(f32[2048]{0:T(1024)} %param.31) | copy-start | bytes 24580
Sparse Core Ops, SparseCore 0:
  10.1 249.3 all-gather.1

commit v3 on v2

--- a/solution.py
+++ b/solution.py
@@ -70,9 +70,16 @@
     feat_cols = feature_weight.shape[1]
     head_size = feat_cols // head_count
     state_size = state_weight.shape[1] // 2
+    seq_count = lax.axis_size("seq")
+    dp_count = lax.axis_size("dp")
+    block_rows = feature_weight.shape[0]
     weights = jnp.concatenate([feature_weight, state_weight, step_weight], axis=1)
-    gathered = lax.all_gather(weights, ("seq", "dp"), axis=0, tiled=True)
-    proj = jnp.dot(features, gathered, preferred_element_type=jnp.float32).astype(jnp.bfloat16)
+    gathered = lax.all_gather(weights, "seq", axis=0, tiled=True)
+    parts = features.reshape(row_count, seq_count, dp_count, block_rows).transpose(2, 0, 1, 3)
+    mine = lax.all_to_all(parts, "dp", 0, 0, tiled=True)
+    mine = mine.reshape(dp_count * row_count, seq_count * block_rows)
+    partial = jnp.dot(mine, gathered, preferred_element_type=jnp.float32)
+    proj = lax.psum_scatter(partial, "dp", scatter_dimension=0, tiled=True).astype(jnp.bfloat16)
     x_proj = proj[:, :feat_cols]
     bc_proj = proj[:, feat_cols : feat_cols + 2 * state_size]
     step_raw = proj[:, feat_cols + 2 * state_size :]

time: 361 us -> 358 us (level)
  waiting for transfers between devices: 258 us -> 220 us
  blocking collectives: 14.2 us -> 41.5 us
  local copies, waits for them, and re-layouts: 13.2 us -> 18.5 us
    all_gather x1, waiting for transfers between devices: 130 us -> 0.02 us  [per_device(): gathered = lax.all_gather(weights, 'seq', axis=0, tiled=True)]
    reduce_scatter x0 -> x1, waiting for transfers between devices: none -> 85.2 us  [per_device(): lax.psum_scatter(partial, 'dp', scatter_dimension=0, tiled=True)]
    all_to_all x0 -> x1, blocking collectives: none -> 27.3 us  [per_device(): mine = lax.all_to_all(parts, 'dp', 0, 0, tiled=True)]
    all_to_all x1, waiting for transfers between devices: 96 us -> 101 us  [per_device(): lax.all_to_all(rows, 'seq', 0, 0, tiled=True).reshape(row_count, width)]
    reshape x0 -> x2, local copies, waits for them, and re-layouts: none -> 4.13 us  [per_device(): features.reshape(row_count, seq_count, dp_count, block_rows)]
  transfers between devices with their start and end apart: 8 -> 9, of which waited for: 7 -> 7; matrix products, arithmetic and copies ran while one was open for 7% -> 9% of each run, Pallas kernels for 0% -> 0%
where the time goes in v3:
time: 358 us; the launch traced here: 356 us
  waiting for transfers between devices  220 us (61%)
  blocking collectives  41.5 us (12%)
  matrix products  22 us (6%)
  starting transfers between devices  21.6 us (6%)
  other arithmetic  18.7 us (5%)
  local copies, waits for them, and re-layouts  18.5 us (5%)
  between operations  14.4 us (4%)
    all_to_all x1, waiting for transfers between devices, per_device(): lax.all_to_all(rows, 'seq', 0, 0, tiled=True).reshape(row_count, width)  101 us
    reduce_scatter x1, waiting for transfers between devices, per_device(): lax.psum_scatter(partial, 'dp', scatter_dimension=0, tiled=True)  85.2 us
    ppermute x6, waiting for transfers between devices, shift(): return (lax.ppermute(x, axis, pairs), reached)  33.2 us
    all_to_all x1, blocking collectives, per_device(): mine = lax.all_to_all(parts, 'dp', 0, 0, tiled=True)  27.3 us
    ppermute x6, starting transfers between devices, shift(): return (lax.ppermute(x, axis, pairs), reached)  18 us
    all_to_all x1, blocking collectives, per_device(): lax.all_to_all(positions[0].reshape(shards, slot), 'seq', 0, 0, tiled=True)  11.7 us
    dot_general x1, matrix products, per_device(): partial = jnp.dot(mine, gathered, preferred_element_type=jnp.float32)  9.63 us
  transfers between devices with their start and end apart: 9, of which 7 were waited for; matrix products, arithmetic and copies ran while one was open for 9% of the time, Pallas kernels for 0%

profile of v3, /device:TPU:0, one launch (start us, length us, event | category | flops | bytes accessed | tf_op | source)
XLA Modules:
  0.0 356.5 jit_solution(3536830504886667757)
XLA Ops:
  7.4 2.4 pad_maximum_fusion
  11.1 11.7 %all_to_all.19 = s32[4,1,64]{2,1,0:T(1,128)S(1)} all-to-all(s32[4,1,64]{2,1,0:T(1,128)S(1)} %all_to_all.13), channel_id=1, replica_groups=mesh['grp'=1,'seq'=4,'dp'=4,'head'=2] {'seq'}, dimensions={0} | all-to-all | bytes 2048 | tf_op jit(solution)/shard_map/all_to_all | solution.py:60
  22.8 3.6 %all-to-all-start = ((bf16[4,64,4096]{2,1,0:T(8,128)(2,1)}), bf16[4,64,4096]{2,1,0:T(8,128)(2,1)S(1)}, u32[]{:S(2)}, u32[]{:S(2)}) async-start(bf16[4,64,4096]{2,1,0:T(8,128)(2,1)} %bitcast.104), calls=%async_computation | async-start | bytes 4194304 | tf_op jit(solution)/shard_map/all_to_all | solution.py:59
  26.6 1.4 scatter_custom_fusion
  28.0 101.3 %all-to-all-done = bf16[4,64,4096]{2,1,0:T(8,128)(2,1)S(1)} async-done(((bf16[4,64,4096]{2,1,0:T(8,128)(2,1)}), bf16[4,64,4096]{2,1,0:T(8,128)(2,1)S(1)}, u32[]{:S(2)}, u32[]{:S(2)}) %all-to-all-start) | async-done | bytes 2097184 | tf_op jit(solution)/shard_map/all_to_all | solution.py:59
  129.3 3.2 gather_fusion
  132.5 3.3 reshape.405
  136.6 27.3 %all_to_all.20 = bf16[4,256,4,256]{3,2,1,0:T(4,128)(2,1)S(1)} all-to-all(bf16[4,256,4,256]{3,2,1,0:T(4,128)(2,1)S(1)} %bitcast.97), channel_id=1, replica_groups=mesh['grp'=1,'seq'=4,'dp'=4,'head'=2] {'dp'}, dimensions={0} | all-to-all | bytes 4194304 | tf_op jit(solution)/shard_map/all_to_all | solution.py:79
  164.4 9.6 %fusion.53 = f32[1024,2192]{0,1:T(8,128)} fusion(bf16[1024,1024]{1,0:T(8,128)(2,1)S(1)} %bitcast.105, bf16[1024,2192]{1,0:T(8,128)(2,1)} %all-gather.2.cloned.1.call-done), kind=kOutput, calls=%fused_computation.100 | convolution fusion | flops 4596957184 | bytes 15564800 | tf_op jit(solution)/shard_map/dot_general | solution.py:81
  177.3 85.2 %reduce-scatter.2.cloned.1.call-done = f32[256,2192]{0,1:T(8,128)} async-done(((f32[1024,2192]{0,1:T(8,128)}), f32[256,2192]{0,1:T(8,128)}) %reduce-scatter.2.cloned.1.call-update) | async-done | bytes 2244624 | tf_op jit(solution)/shard_map/reduce_scatter | solution.py:82
  262.5 1.7 convert_element_type.43
  265.6 1.3 fusion.8
  266.9 1.3 fusion.9
  269.4 3.4 collective-permute-start
  273.6 1.3 collective-permute-start.3
  275.1 9.1 %collective-permute-done = f32[1032,128]{1,0:T(8,128)S(1)} collective-permute-done((f32[1032,128]{1,0:T(8,128)}, f32[1032,128]{1,0:T(8,128)S(1)}, u32[]{:S(2)}, u32[]{:S(2)}) %collective-permute-start) | collective-permute-done | bytes 528416 | tf_op jit(solution)/shard_map/ppermute | solution.py:23
  284.8 4.5 %collective-permute-start.1 = (f32[1032,128]{1,0:T(8,128)S(1)}, f32[1032,128]{1,0:T(8,128)S(1)}, u32[]{:S(2)}, u32[]{:S(2)}) collective-permute-start(f32[1032,128]{1,0:T(8,128)S(1)} %scatter.26), channel_id=1, source_target_pairs={{0,8},{8,16},{16,24},{1,9},{9,17},{17,25},{2,10},{10,18},{18,26},{... | collective-permute-start | bytes 1585160 | tf_op jit(solution)/shard_map/ppermute | solution.py:23
  289.3 5.6 %fusion = f32[16,128,256]{2,1,0:T(8,128)} fusion(bf16[256,16,128]{0,2,1:T(8,128)(2,1)S(1)} %bitcast.94, f32[16,256]{1,0:T(8,128)S(1)} %get-tuple-element.81, f32[256,256]{1,0:T(8,128)} %fusion.35, f32[16,256]{1,0:T(8,128)S(1)} %get-tuple-element.91, f32[256,256]{1,0:T(8,128)S(1)} %fusion.42), kind=kOutput, calls=%fused_computation.2 | convolution fusion | flops 1616904192 | bytes 3702784 | tf_op jit(solution)/shard_map/hts,shp->thp/dot_general | solution.py:105
  295.6 1.3 scatter.30
  296.9 1.3 collective-permute-start.4
  300.3 1.4 multiply_add_fusion.1
  302.6 6.2 %collective-permute-start.2 = (f32[1032,128]{1,0:T(8,128)}, f32[1032,128]{1,0:T(8,128)}, u32[]{:S(2)}, u32[]{:S(2)}) collective-permute-start(f32[1032,128]{1,0:T(8,128)} %pad_maximum_fusion.1), channel_id=1, source_target_pairs={{0,16},{8,24},{1,17},{9,25},{2,18},{10,26},{3,19},{11,27},{4,20},{... | collective-permute-start | bytes 1585160 | tf_op jit(solution)/shard_map/ppermute | solution.py:23
  308.8 2.8 collective-permute-done.4
  312.5 1.4 multiply_add_fusion
  314.0 1.3 collective-permute-start.5
  316.7 1.2 collective-permute-done.2
  319.0 1.3 fusion.25
  320.3 19.5 %collective-permute-done.5 = f32[1032,128]{1,0:T(8,128)S(1)} collective-permute-done((f32[1032,128]{1,0:T(8,128)S(1)}, f32[1032,128]{1,0:T(8,128)S(1)}, u32[]{:S(2)}, u32[]{:S(2)}) %collective-permute-start.5) | collective-permute-done | bytes 528416 | tf_op jit(solution)/shard_map/ppermute | solution.py:23
  339.9 2.6 multiply_reduce_fusion
  342.5 1.9 copy.36
  344.4 2.4 psum.7
  346.8 2.8 multiply_convert_fusion
  (84 shorter events, 17.3 us)
Async XLA Ops:
  6.5 3.8 %copy-start.8 = (s32[1,256]{1,0:T(1,128)S(1)}, s32[1,256]{1,0:T(1,128)}, u32[]{:S(2)}) copy-start(s32[1,256]{1,0:T(1,128)} %param.23) | copy-start | bytes 3076
  6.5 157.9 %all-gather.2.cloned.1.call-start = ((), (), s32[]{:S(2)}) async-start(), calls=%async_computation.4 | async-start | bytes 5898240 | tf_op jit(solution)/shard_map/all_gather | solution.py:77
  22.8 106.5 %all-to-all-start = ((bf16[4,64,4096]{2,1,0:T(8,128)(2,1)}), bf16[4,64,4096]{2,1,0:T(8,128)(2,1)S(1)}, u32[]{:S(2)}, u32[]{:S(2)}) async-start(bf16[4,64,4096]{2,1,0:T(8,128)(2,1)} %bitcast.104), calls=%async_computation | async-start | bytes 4194304 | tf_op jit(solution)/shard_map/all_to_all | solution.py:59
  26.4 236.1 %reduce-scatter.2.cloned.1.call-start = ((), (), s32[]{:S(2)}) async-start(), calls=%async_computation.5 | async-start | bytes 11223040 | tf_op jit(solution)/shard_map/reduce_scatter | solution.py:82
  174.1 0.7 copy-start.9
  174.1 2.5 copy-start.11
  177.3 87.1 %copy-start.7 = (f32[16]{0:T(128)S(1)}, f32[16]{0:T(128)}, u32[]{:S(2)}) copy-start(f32[16]{0:T(128)} %param.28) | copy-start | bytes 196
  264.2 54.7 %copy-start = (bf16[256,2192]{0,1:T(8,128)(2,1)}, bf16[256,2192]{0,1:T(8,128)(2,1)S(1)}, u32[]{:S(2)}) copy-start(bf16[256,2192]{0,1:T(8,128)(2,1)S(1)} %convert_element_type.43) | copy-start | bytes 3366916
  269.4 14.8 %collective-permute-start = (f32[1032,128]{1,0:T(8,128)}, f32[1032,128]{1,0:T(8,128)S(1)}, u32[]{:S(2)}, u32[]{:S(2)}) collective-permute-start(f32[1032,128]{1,0:T(8,128)} %get-tuple-element.95), channel_id=1, source_target_pairs={{0,8},{8,16},{16,24},{1,9},{9,17},{17,25},{2,10},{10,18},{18,26},{... | collective-permute-start | bytes 1585160 | tf_op jit(solution)/shard_map/ppermute | solution.py:23
  273.6 21.3 %collective-permute-start.3 = (f32[1032,128]{1,0:T(8,128)}, f32[1032,128]{1,0:T(8,128)}, u32[]{:S(2)}, u32[]{:S(2)}) collective-permute-start(f32[1032,128]{1,0:T(8,128)} %get-tuple-element.94), channel_id=1, source_target_pairs={{8,0},{16,8},{24,16},{9,1},{17,9},{25,17},{10,2},{18,10},{26,18},{... | collective-permute-start | bytes 1585160 | tf_op jit(solution)/shard_map/ppermute | solution.py:23
  284.2 0.6 copy-start.5
  284.8 10.1 %copy-start.2 = (f32[1032,128]{1,0:T(8,128)}, f32[1032,128]{1,0:T(8,128)S(1)}, u32[]{:S(2)}) copy-start(f32[1032,128]{1,0:T(8,128)S(1)} %scatter.26) | copy-start | bytes 1585156
  284.8 14.6 %collective-permute-start.1 = (f32[1032,128]{1,0:T(8,128)S(1)}, f32[1032,128]{1,0:T(8,128)S(1)}, u32[]{:S(2)}, u32[]{:S(2)}) collective-permute-start(f32[1032,128]{1,0:T(8,128)S(1)} %scatter.26), channel_id=1, source_target_pairs={{0,8},{8,16},{16,24},{1,9},{9,17},{17,25},{2,10},{10,18},{18,26},{... | collective-permute-start | bytes 1585160 | tf_op jit(solution)/shard_map/ppermute | solution.py:23
  296.9 14.8 %collective-permute-start.4 = (f32[1032,128]{1,0:T(8,128)}, f32[1032,128]{1,0:T(8,128)}, u32[]{:S(2)}, u32[]{:S(2)}) collective-permute-start(f32[1032,128]{1,0:T(8,128)} %scatter.30), channel_id=1, source_target_pairs={{8,0},{16,8},{24,16},{9,1},{17,9},{25,17},{10,2},{18,10},{26,18},{... | collective-permute-start | bytes 1585160 | tf_op jit(solution)/shard_map/ppermute | solution.py:23
  299.4 0.8 copy-start.3
  302.6 12.7 %copy-start.6 = (f32[1,128]{1,0:T(1,128)S(1)}, f32[1,128]{1,0:T(1,128)}, u32[]{:S(2)}) copy-start(f32[1,128]{1,0:T(1,128)} %copy-done.5) | copy-start | bytes 1540
  302.6 15.3 %collective-permute-start.2 = (f32[1032,128]{1,0:T(8,128)}, f32[1032,128]{1,0:T(8,128)}, u32[]{:S(2)}, u32[]{:S(2)}) collective-permute-start(f32[1032,128]{1,0:T(8,128)} %pad_maximum_fusion.1), channel_id=1, source_target_pairs={{0,16},{8,24},{1,17},{9,25},{2,18},{10,26},{3,19},{11,27},{4,20},{... | collective-permute-start | bytes 1585160 | tf_op jit(solution)/shard_map/ppermute | solution.py:23
  314.0 25.8 %collective-permute-start.5 = (f32[1032,128]{1,0:T(8,128)S(1)}, f32[1032,128]{1,0:T(8,128)S(1)}, u32[]{:S(2)}, u32[]{:S(2)}) collective-permute-start(f32[1032,128]{1,0:T(8,128)S(1)} %pad_maximum_fusion.2), channel_id=1, source_target_pairs={{16,0},{24,8},{17,1},{25,9},{18,2},{26,10},{19,3},{27,11},{20,4},{... | collective-permute-start | bytes 1585160 | tf_op jit(solution)/shard_map/ppermute | solution.py:23
  319.0 20.9 %copy-start.1 = (f32[16,128,256]{2,1,0:T(8,128)S(1)}, f32[16,128,256]{2,1,0:T(8,128)}, u32[]{:S(2)}) copy-start(f32[16,128,256]{2,1,0:T(8,128)} %fusion) | copy-start | bytes 6291460
  319.0 20.9 %copy-start.10 = (f32[16]{0:T(128)S(1)}, f32[16]{0:T(128)}, u32[]{:S(2)}) copy-start(f32[16]{0:T(128)} %param.30) | copy-start | bytes 196
  342.5 4.3 %copy-start.4 = (f32[2048]{0:T(1024)S(1)}, f32[2048]{0:T(1024)}, u32[]{:S(2)}) copy-start(f32[2048]{0:T(1024)} %param.31) | copy-start | bytes 24580
Sparse Core Ops, SparseCore 0:
  9.9 136.5 all-gather.1
  174.2 88.2 reduce-scatter.1

commit v4 on v2

--- a/solution.py
+++ b/solution.py
@@ -51,12 +51,26 @@
     norm_gain,
 ):
     row_count = tokens_in.shape[1]
-    width = tokens_in.shape[2]
     shards = lax.axis_size("seq")
     here = lax.axis_index("seq")
     slot = row_count // shards
-    rows = tokens_in[0].reshape(shards, slot, width)
-    moved_rows = lax.all_to_all(rows, "seq", 0, 0, tiled=True).reshape(row_count, width)
+    head_count = step_bias.shape[0]
+    feat_cols = feature_weight.shape[1]
+    head_size = feat_cols // head_count
+    state_size = state_weight.shape[1] // 2
+
+    seq_count = lax.axis_size("seq")
+    dp_count = lax.axis_size("dp")
+    block_rows = feature_weight.shape[0]
+    weights = jnp.concatenate([feature_weight, state_weight, step_weight], axis=1)
+    gathered = lax.all_gather(weights, "seq", axis=0, tiled=True)
+    parts = tokens_in[0].reshape(row_count, seq_count, dp_count, block_rows).transpose(2, 0, 1, 3)
+    mine = lax.all_to_all(parts, "dp", 0, 0, tiled=True)
+    mine = mine.reshape(dp_count * row_count, seq_count * block_rows)
+    partial = jnp.dot(mine, gathered, preferred_element_type=jnp.float32)
+    projected = lax.psum_scatter(partial, "dp", scatter_dimension=0, tiled=True)
+    projected = projected.astype(jnp.bfloat16).reshape(shards, slot, -1)
+    moved = lax.all_to_all(projected, "seq", 0, 0, tiled=True).reshape(row_count, -1)
     moved_positions = lax.all_to_all(
         positions[0].reshape(shards, slot), "seq", 0, 0, tiled=True
     ).reshape(row_count)
@@ -64,15 +78,7 @@
     inverse = jnp.zeros((row_count,), jnp.int32).at[offsets].set(
         jnp.arange(row_count, dtype=jnp.int32)
     )
-    features = moved_rows[inverse]
-
-    head_count = step_bias.shape[0]
-    feat_cols = feature_weight.shape[1]
-    head_size = feat_cols // head_count
-    state_size = state_weight.shape[1] // 2
-    weights = jnp.concatenate([feature_weight, state_weight, step_weight], axis=1)
-    gathered = lax.all_gather(weights, ("seq", "dp"), axis=0, tiled=True)
-    proj = jnp.dot(features, gathered, preferred_element_type=jnp.float32).astype(jnp.bfloat16)
+    proj = moved[inverse]
     x_proj = proj[:, :feat_cols]
     bc_proj = proj[:, feat_cols : feat_cols + 2 * state_size]
     step_raw = proj[:, feat_cols + 2 * state_size :]

time: 361 us -> 329 us (0.911)
  waiting for transfers between devices: 258 us -> 196 us
  blocking collectives: 14.2 us -> 32.8 us
  starting transfers between devices: 21.5 us -> 26.7 us
    reduce_scatter x0 -> x1, waiting for transfers between devices: none -> 84.5 us  [per_device(): projected = lax.psum_scatter(partial, 'dp', scatter_dimension=0, tiled=True)]
    all_gather x1, waiting for transfers between devices: 130 us -> 57.2 us  [per_device(): gathered = lax.all_gather(weights, 'seq', axis=0, tiled=True)]
    all_to_all x1 -> x2, waiting for transfers between devices: 96 us -> 24.3 us  [the longest x1 24.3 us: per_device(): lax.all_to_all(projected, 'seq', 0, 0, tiled=True).reshape(row_count, -1)]
    all_to_all x1, blocking collectives: 11.7 us -> 30.4 us  [per_device(): mine = lax.all_to_all(parts, 'dp', 0, 0, tiled=True)]
    another operation x4 -> x6, local copies, waits for them, and re-layouts: 0.36 us -> 4.49 us  [the longest x2 4.13 us: per_device(): tokens_in[0].reshape(row_count, seq_count, dp_count, block_rows)]
    all_to_all x1 -> x2, starting transfers between devices: 3.74 us -> 7.82 us  [the longest x1 4.59 us: per_device(): lax.all_to_all(projected, 'seq', 0, 0, tiled=True).reshape(row_count, -1)]
  transfers between devices with their start and end apart: 8 -> 10, of which waited for: 7 -> 8; matrix products, arithmetic and copies ran while one was open for 7% -> 8% of each run, Pallas kernels for 0% -> 0%
where the time goes in v4:
time: 329 us; the launch traced here: 328 us
  waiting for transfers between devices  196 us (60%)
  blocking collectives  32.8 us (10%)
  starting transfers between devices  26.7 us (8%)
  matrix products  22.3 us (7%)
  other arithmetic  19.3 us (6%)
  local copies, waits for them, and re-layouts  16.5 us (5%)
  between operations  14.4 us (4%)
    reduce_scatter x1, waiting for transfers between devices, per_device(): projected = lax.psum_scatter(partial, 'dp', scatter_dimension=0, tiled=True)  84.5 us
    all_gather x1, waiting for transfers between devices, per_device(): gathered = lax.all_gather(weights, 'seq', axis=0, tiled=True)  57.2 us
    all_to_all x1, blocking collectives, per_device(): mine = lax.all_to_all(parts, 'dp', 0, 0, tiled=True)  30.4 us
    ppermute x6, waiting for transfers between devices, shift(): return (lax.ppermute(x, axis, pairs), reached)  30.3 us
    all_to_all x1, waiting for transfers between devices, per_device(): lax.all_to_all(projected, 'seq', 0, 0, tiled=True).reshape(row_count, -1)  24.3 us
    ppermute x6, starting transfers between devices, shift(): return (lax.ppermute(x, axis, pairs), reached)  18.8 us
    dot_general x1, matrix products, per_device(): partial = jnp.dot(mine, gathered, preferred_element_type=jnp.float32)  9.96 us
  transfers between devices with their start and end apart: 10, of which 8 were waited for; matrix products, arithmetic and copies ran while one was open for 8% of the time, Pallas kernels for 0%

profile of v4, /device:TPU:0, one launch (start us, length us, event | category | flops | bytes accessed | tf_op | source)
XLA Modules:
  0.0 328.4 jit_solution(13691790862936015671)
XLA Ops:
  7.4 2.4 pad_maximum_fusion
  9.8 3.3 %reshape_squeeze.4 = bf16[256,4,4,256]{3,2,1,0:T(4,128)(2,1)S(1)} reshape(bf16[1,256,4096]{2,1,0:T(8,128)(2,1)} %param.22) | data formatting | bytes 4194304 | tf_op jit(solution)/shard_map/reshape;squeeze | solution.py:67
  13.9 30.4 %all_to_all.19 = bf16[4,256,4,256]{3,2,1,0:T(4,128)(2,1)S(1)} all-to-all(bf16[4,256,4,256]{3,2,1,0:T(4,128)(2,1)S(1)} %bitcast.103), channel_id=1, replica_groups=mesh['grp'=1,'seq'=4,'dp'=4,'head'=2] {'dp'}, dimensions={0} | all-to-all | bytes 4194304 | tf_op jit(solution)/shard_map/all_to_all | solution.py:68
  44.8 57.2 %all-gather.2.cloned.1.call-done = bf16[1024,2192]{1,0:T(8,128)(2,1)} async-done(((bf16[256,2192]{1,0:T(8,128)(2,1)}), bf16[1024,2192]{1,0:T(8,128)(2,1)}) %all-gather.2.cloned.1.call-update) | async-done | bytes 4489232 | tf_op jit(solution)/shard_map/all_gather | solution.py:66
  102.0 10.0 %convolution_bitcast_fusion = f32[1024,2192]{0,1:T(8,128)} fusion(bf16[1024,2192]{1,0:T(8,128)(2,1)} %all-gather.2.cloned.1.call-done, bf16[1024,1024]{1,0:T(8,128)(2,1)S(1)} %bitcast.110), kind=kOutput, calls=%fused_computation.2 | convolution fusion | flops 4596957184 | bytes 15564800 | tf_op jit(solution)/shard_map/dot_general | solution.py:70
  114.0 3.2 all-to-all-start.2
  117.2 84.5 %reduce-scatter.2.cloned.1.call-done = f32[256,2192]{0,1:T(8,128)} async-done(((f32[1024,2192]{0,1:T(8,128)}), f32[256,2192]{0,1:T(8,128)}) %reduce-scatter.2.cloned.1.call-update) | async-done | bytes 2244624 | tf_op jit(solution)/shard_map/reduce_scatter | solution.py:71
  201.7 1.7 convert_element_type.43
  203.5 1.5 copy.77
  205.0 4.6 %all-to-all-start.1 = ((bf16[4,64,2192]{2,1,0:T(8,128)(2,1)}), bf16[4,64,2192]{2,1,0:T(8,128)(2,1)S(1)}, u32[]{:S(2)}, u32[]{:S(2)}) async-start(bf16[4,64,2192]{2,1,0:T(8,128)(2,1)} %bitcast.2), calls=%async_computation.2 | async-start | bytes 2359296 | tf_op jit(solution)/shard_map/all_to_all | solution.py:73
  212.3 1.4 scatter_custom_fusion
  213.7 24.3 %all-to-all-done.1 = bf16[4,64,2192]{2,1,0:T(8,128)(2,1)S(1)} async-done(((bf16[4,64,2192]{2,1,0:T(8,128)(2,1)}), bf16[4,64,2192]{2,1,0:T(8,128)(2,1)S(1)}, u32[]{:S(2)}, u32[]{:S(2)}) %all-to-all-start.1) | async-done | bytes 1122336 | tf_op jit(solution)/shard_map/all_to_all | solution.py:73
  238.0 1.4 gather_fusion
  242.7 1.3 fusion.9
  244.1 1.3 fusion.8
  246.4 1.3 collective-permute-start.3
  247.7 4.6 %collective-permute-start = (f32[1032,128]{1,0:T(8,128)}, f32[1032,128]{1,0:T(8,128)S(1)}, u32[]{:S(2)}, u32[]{:S(2)}) collective-permute-start(f32[1032,128]{1,0:T(8,128)} %get-tuple-element.95), channel_id=1, source_target_pairs={{0,8},{8,16},{16,24},{1,9},{9,17},{17,25},{2,10},{10,18},{18,26},{... | collective-permute-start | bytes 1585160 | tf_op jit(solution)/shard_map/ppermute | solution.py:23
  253.3 8.2 %collective-permute-done.3 = f32[1032,128]{1,0:T(8,128)S(1)} collective-permute-done((f32[1032,128]{1,0:T(8,128)}, f32[1032,128]{1,0:T(8,128)S(1)}, u32[]{:S(2)}, u32[]{:S(2)}) %collective-permute-start.3) | collective-permute-done | bytes 528416 | tf_op jit(solution)/shard_map/ppermute | solution.py:23
  261.6 1.3 collective-permute-start.4
  263.0 5.3 %collective-permute-start.1 = (f32[1032,128]{1,0:T(8,128)S(1)}, f32[1032,128]{1,0:T(8,128)}, u32[]{:S(2)}, u32[]{:S(2)}) collective-permute-start(f32[1032,128]{1,0:T(8,128)S(1)} %scatter.26), channel_id=1, source_target_pairs={{0,8},{8,16},{16,24},{1,9},{9,17},{17,25},{2,10},{10,18},{18,26},{... | collective-permute-start | bytes 1585160 | tf_op jit(solution)/shard_map/ppermute | solution.py:23
  268.3 5.7 %fusion = f32[16,128,256]{2,1,0:T(8,128)} fusion(bf16[256,16,128]{0,2,1:T(8,128)(2,1)S(1)} %bitcast.100, f32[16,256]{1,0:T(8,128)} %get-tuple-element.91, f32[256,256]{1,0:T(8,128)} %fusion.35, f32[16,256]{1,0:T(8,128)} %get-tuple-element.90, f32[256,256]{1,0:T(8,128)S(1)} %fusion.41), kind=kOutput, calls=%fused_computation.3 | convolution fusion | flops 1616904192 | bytes 3702784 | tf_op jit(solution)/shard_map/hts,shp->thp/dot_general | solution.py:104
  274.0 1.8 collective-permute-done.4
  277.8 1.4 multiply_add_fusion.1
  280.1 5.0 %collective-permute-start.2 = (f32[1032,128]{1,0:T(8,128)}, f32[1032,128]{1,0:T(8,128)}, u32[]{:S(2)}, u32[]{:S(2)}) collective-permute-start(f32[1032,128]{1,0:T(8,128)} %pad_maximum_fusion.1), channel_id=1, source_target_pairs={{0,16},{8,24},{1,17},{9,25},{2,18},{10,26},{3,19},{11,27},{4,20},{... | collective-permute-start | bytes 1585160 | tf_op jit(solution)/shard_map/ppermute | solution.py:23
  285.2 1.4 multiply_add_fusion
  286.7 1.3 collective-permute-start.5
  289.3 4.2 %collective-permute-done.2 = f32[1032,128]{1,0:T(8,128)} collective-permute-done((f32[1032,128]{1,0:T(8,128)}, f32[1032,128]{1,0:T(8,128)}, u32[]{:S(2)}, u32[]{:S(2)}) %collective-permute-start.2) | collective-permute-done | bytes 528416 | tf_op jit(solution)/shard_map/ppermute | solution.py:23
  295.8 15.8 %collective-permute-done.5 = f32[1032,128]{1,0:T(8,128)S(1)} collective-permute-done((f32[1032,128]{1,0:T(8,128)S(1)}, f32[1032,128]{1,0:T(8,128)S(1)}, u32[]{:S(2)}, u32[]{:S(2)}) %collective-permute-start.5) | collective-permute-done | bytes 528416 | tf_op jit(solution)/shard_map/ppermute | solution.py:23
  311.7 2.6 multiply_reduce_fusion
  314.4 1.9 copy.88
  316.3 2.4 psum.7
  318.7 2.8 multiply_convert_fusion
  (89 shorter events, 18.3 us)
Async XLA Ops:
  6.5 95.5 %all-gather.2.cloned.1.call-start = ((), (), s32[]{:S(2)}) async-start(), calls=%async_computation.4 | async-start | bytes 5898240 | tf_op jit(solution)/shard_map/all_gather | solution.py:66
  9.7 192.0 %reduce-scatter.2.cloned.1.call-start = ((), (), s32[]{:S(2)}) async-start(), calls=%async_computation.5 | async-start | bytes 11223040 | tf_op jit(solution)/shard_map/reduce_scatter | solution.py:71
  112.0 0.7 copy-start.8
  114.0 91.0 %all-to-all-start.2 = ((s32[4,1,64]{2,1,0:T(1,128)}), s32[4,1,64]{2,1,0:T(1,128)S(1)}, u32[]{:S(2)}, u32[]{:S(2)}) async-start(s32[4,1,64]{2,1,0:T(1,128)} %all_to_all.14), calls=%async_computation.3 | async-start | bytes 4096 | tf_op jit(solution)/shard_map/all_to_all | solution.py:74
  203.5 6.2 %copy-start.9 = (s32[1,256]{1,0:T(1,128)S(1)}, s32[1,256]{1,0:T(1,128)}, u32[]{:S(2)}) copy-start(s32[1,256]{1,0:T(1,128)} %param.24) | copy-start | bytes 3076
  203.5 8.0 %copy-start.11 = (f32[16]{0:T(128)S(1)}, f32[16]{0:T(128)}, u32[]{:S(2)}) copy-start(f32[16]{0:T(128)} %param.29) | copy-start | bytes 196
  205.0 33.0 %all-to-all-start.1 = ((bf16[4,64,2192]{2,1,0:T(8,128)(2,1)}), bf16[4,64,2192]{2,1,0:T(8,128)(2,1)S(1)}, u32[]{:S(2)}, u32[]{:S(2)}) async-start(bf16[4,64,2192]{2,1,0:T(8,128)(2,1)} %bitcast.2), calls=%async_computation.2 | async-start | bytes 2359296 | tf_op jit(solution)/shard_map/all_to_all | solution.py:73
  239.4 55.2 %copy-start = (bf16[256,2192]{1,0:T(8,128)(2,1)}, bf16[256,2192]{1,0:T(8,128)(2,1)S(1)}, u32[]{:S(2)}) copy-start(bf16[256,2192]{1,0:T(8,128)(2,1)S(1)} %gather_fusion) | copy-start | bytes 3366916
  239.4 0.7 copy-start.7
  246.4 15.1 %collective-permute-start.3 = (f32[1032,128]{1,0:T(8,128)}, f32[1032,128]{1,0:T(8,128)S(1)}, u32[]{:S(2)}, u32[]{:S(2)}) collective-permute-start(f32[1032,128]{1,0:T(8,128)} %get-tuple-element.94), channel_id=1, source_target_pairs={{8,0},{16,8},{24,16},{9,1},{17,9},{25,17},{10,2},{18,10},{26,18},{... | collective-permute-start | bytes 1585160 | tf_op jit(solution)/shard_map/ppermute | solution.py:23
  247.7 15.2 %collective-permute-start = (f32[1032,128]{1,0:T(8,128)}, f32[1032,128]{1,0:T(8,128)S(1)}, u32[]{:S(2)}, u32[]{:S(2)}) collective-permute-start(f32[1032,128]{1,0:T(8,128)} %get-tuple-element.95), channel_id=1, source_target_pairs={{0,8},{8,16},{16,24},{1,9},{9,17},{17,25},{2,10},{10,18},{18,26},{... | collective-permute-start | bytes 1585160 | tf_op jit(solution)/shard_map/ppermute | solution.py:23
  261.6 12.4 %copy-start.3 = (f32[1032,128]{1,0:T(8,128)}, f32[1032,128]{1,0:T(8,128)S(1)}, u32[]{:S(2)}) copy-start(f32[1032,128]{1,0:T(8,128)S(1)} %scatter.30) | copy-start | bytes 1585156
  261.6 14.2 %collective-permute-start.4 = (f32[1032,128]{1,0:T(8,128)S(1)}, f32[1032,128]{1,0:T(8,128)}, u32[]{:S(2)}, u32[]{:S(2)}) collective-permute-start(f32[1032,128]{1,0:T(8,128)S(1)} %scatter.30), channel_id=1, source_target_pairs={{8,0},{16,8},{24,16},{9,1},{17,9},{25,17},{10,2},{18,10},{26,18},{... | collective-permute-start | bytes 1585160 | tf_op jit(solution)/shard_map/ppermute | solution.py:23
  263.0 11.0 %copy-start.2 = (f32[1032,128]{1,0:T(8,128)}, f32[1032,128]{1,0:T(8,128)S(1)}, u32[]{:S(2)}) copy-start(f32[1032,128]{1,0:T(8,128)S(1)} %scatter.26) | copy-start | bytes 1585156
  263.0 14.0 %collective-permute-start.1 = (f32[1032,128]{1,0:T(8,128)S(1)}, f32[1032,128]{1,0:T(8,128)}, u32[]{:S(2)}, u32[]{:S(2)}) collective-permute-start(f32[1032,128]{1,0:T(8,128)S(1)} %scatter.26), channel_id=1, source_target_pairs={{0,8},{8,16},{16,24},{1,9},{9,17},{17,25},{2,10},{10,18},{18,26},{... | collective-permute-start | bytes 1585160 | tf_op jit(solution)/shard_map/ppermute | solution.py:23
  280.1 13.4 %collective-permute-start.2 = (f32[1032,128]{1,0:T(8,128)}, f32[1032,128]{1,0:T(8,128)}, u32[]{:S(2)}, u32[]{:S(2)}) collective-permute-start(f32[1032,128]{1,0:T(8,128)} %pad_maximum_fusion.1), channel_id=1, source_target_pairs={{0,16},{8,24},{1,17},{9,25},{2,18},{10,26},{3,19},{11,27},{4,20},{... | collective-permute-start | bytes 1585160 | tf_op jit(solution)/shard_map/ppermute | solution.py:23
  286.7 25.0 %collective-permute-start.5 = (f32[1032,128]{1,0:T(8,128)S(1)}, f32[1032,128]{1,0:T(8,128)S(1)}, u32[]{:S(2)}, u32[]{:S(2)}) collective-permute-start(f32[1032,128]{1,0:T(8,128)S(1)} %pad_maximum_fusion.2), channel_id=1, source_target_pairs={{16,0},{24,8},{17,1},{25,9},{18,2},{26,10},{19,3},{27,11},{20,4},{... | collective-permute-start | bytes 1585160 | tf_op jit(solution)/shard_map/ppermute | solution.py:23
  294.6 17.1 %copy-start.1 = (f32[16,128,256]{2,1,0:T(8,128)S(1)}, f32[16,128,256]{2,1,0:T(8,128)}, u32[]{:S(2)}) copy-start(f32[16,128,256]{2,1,0:T(8,128)} %fusion) | copy-start | bytes 6291460
  294.6 17.1 %copy-start.4 = (f32[256,16]{0,1:T(8,128)S(1)}, f32[256,16]{0,1:T(8,128)}, u32[]{:S(2)}) copy-start(f32[256,16]{0,1:T(8,128)} %get-tuple-element.74) | copy-start | bytes 49156
  294.6 17.1 %copy-start.5 = (f32[256,16]{0,1:T(8,128)S(1)}, f32[256,16]{0,1:T(8,128)}, u32[]{:S(2)}) copy-start(f32[256,16]{0,1:T(8,128)} %get-tuple-element.86) | copy-start | bytes 49156
  294.6 17.1 %copy-start.10 = (f32[16]{0:T(128)S(1)}, f32[16]{0:T(128)}, u32[]{:S(2)}) copy-start(f32[16]{0:T(128)} %param.30) | copy-start | bytes 196
  314.4 4.3 %copy-start.6 = (f32[2048]{0:T(1024)S(1)}, f32[2048]{0:T(1024)}, u32[]{:S(2)}) copy-start(f32[2048]{0:T(1024)} %param.31) | copy-start | bytes 24580
Sparse Core Ops, SparseCore 0:
  9.9 92.0 all-gather.1
  112.1 89.5 reduce-scatter.1
